TPU v7x, 512 devices: a whole 4x4x16 slice. The times are simulated.
512 devices in a mesh: blk: 64 (over y, x, z_hi, core), mp: 8 (over z_lo).
Axes of the slice: x: 4, y: 4, z: 16 (z_hi: 2, z_lo: 8; z = z_hi * 8 + z_lo), core: 2. Of those that a mesh axis runs over, the one named last changes fastest.
Arguments:
- queries: bfloat16 [16384, 5120], P('blk', 'mp'), may hold values from -8.5 to 8.5
- suffix_key_rows: bfloat16 [16384, 1024], P('blk', 'mp'), may hold values from -6 to 6
- suffix_value_rows: bfloat16 [16384, 1024], P('blk', 'mp'), may hold values from -6 to 6
- shared_prefix_keys: bfloat16 [2048, 1024], P('blk', 'mp'), may hold values from -8.5 to 8.5
- shared_prefix_values: bfloat16 [2048, 1024], P('blk', 'mp'), may hold values from -6 to 6
- out_weight: bfloat16 [5120, 5120], P('mp', 'blk'), may hold values from -0.078125 to 0.078125
- lengths: int32 [16], replicated, may hold values from 1 to 4096, 16384 in all
Outputs:
- output: bfloat16 [16384, 5120], P('blk', 'mp')
Inputs may be any that keep to these rules, and one draw needn't show every extreme that they name: The lengths sum to 16384; the longest is exactly 4096.
All inputs are finite; a program needn't handle non-finite values.
Results may differ from a plain program's by a relative error of at most 0.019.
Values may be sent and summed in bfloat16 or wider, within the bound.
No kernel may reach another device: no remote copies, remote signals or barrier semaphores. Data moves between devices by JAX's collectives and lax.ppermute only.
A program may use at most 64 MiB of HBM per device.

v0:
```python
import math
import jax
import jax.numpy as jnp
from jax import lax
from jax.sharding import PartitionSpec as P

HEAD_SIZE = 128
MASKED_SCORE = -1e30


def passed_along(block, axis, distance):
    devices = range(lax.axis_size(axis))
    route = [(i - distance, i) for i in devices if i - distance in devices]
    return lax.ppermute(block, axis, route)


def per_device(
    queries,
    suffix_key_rows,
    suffix_value_rows,
    shared_prefix_keys,
    shared_prefix_values,
    out_weight,
    lengths,
):
    tok_rows = queries.shape[0]
    kv_heads = suffix_key_rows.shape[1] // HEAD_SIZE
    q_heads = queries.shape[1] // HEAD_SIZE
    heads_per_group = q_heads // kv_heads
    blocks = lax.axis_size("blk")
    cycle_reach = blocks // 4
    my_block = lax.axis_index("blk")
    score_scale = 1.0 / math.sqrt(HEAD_SIZE)
    heads_of_query = queries.reshape(tok_rows, kv_heads, heads_per_group, HEAD_SIZE)
    req_ends = jnp.cumsum(lengths)
    local_rows = jnp.arange(tok_rows, dtype=jnp.int32)
    query_pos = my_block * tok_rows + local_rows

    def owner_of(position):
        return jnp.sum((position[:, None] >= req_ends[None, :]).astype(jnp.int32), axis=1)

    query_owner = owner_of(query_pos)

    def update(carry_state, key_block, value_block, visible):
        run_max, row_total, accumulated = carry_state
        count = key_block.shape[0]
        key_heads = key_block.reshape(count, kv_heads, HEAD_SIZE)
        value_heads = value_block.reshape(count, kv_heads, HEAD_SIZE)
        scores = (
            jnp.einsum(
                "qhgd,khd->hgqk", heads_of_query, key_heads, preferred_element_type=jnp.float32
            )
            * score_scale
        )
        if visible is not None:
            scores = jnp.where(visible[None, None], scores, MASKED_SCORE)
        new_max = jnp.maximum(run_max, jnp.max(scores, axis=-1))
        weights = jnp.exp(scores - new_max[..., None])
        if visible is not None:
            weights = jnp.where(visible[None, None], weights, 0.0)
        rescale = jnp.exp(run_max - new_max)
        row_total = row_total * rescale + jnp.sum(weights, axis=-1)
        contrib = jnp.einsum(
            "hgqk,khd->hgqd",
            weights.astype(jnp.bfloat16),
            value_heads,
            preferred_element_type=jnp.float32,
        )
        accumulated = accumulated * rescale[..., None] + contrib
        return (new_max, row_total, accumulated)

    start_state = (
        jnp.full((kv_heads, heads_per_group, tok_rows), MASKED_SCORE, jnp.float32),
        jnp.zeros((kv_heads, heads_per_group, tok_rows), jnp.float32),
        jnp.zeros((kv_heads, heads_per_group, tok_rows, HEAD_SIZE), jnp.float32),
    )
    carry_state = update(
        start_state,
        lax.all_gather(shared_prefix_keys, "blk", axis=0, tiled=True),
        lax.all_gather(shared_prefix_values, "blk", axis=0, tiled=True),
        None,
    )

    def visible_from(distance):
        key_pos = (my_block - distance) * tok_rows + local_rows
        key_owner = owner_of(key_pos)
        return (
            (key_owner[None, :] == query_owner[:, None])
            & (key_pos[None, :] <= query_pos[:, None])
            & (key_pos[None, :] >= 0)
        )

    kv_pair = jnp.stack((suffix_key_rows, suffix_value_rows))
    carry_state = update(carry_state, kv_pair[0], kv_pair[1], visible_from(0))

    def advance(distance, loop_carry):
        current, moving = loop_carry
        moving = passed_along(moving, "blk", 1)
        visible = visible_from(distance)
        current = update(current, moving[0], moving[1], visible)
        return (current, moving)

    carry_state, kv_pair = lax.fori_loop(1, cycle_reach + 1, advance, (carry_state, kv_pair))
    run_max, row_total, accumulated = carry_state
    attended = accumulated / row_total[..., None]
    attn = (
        jnp.transpose(attended, (2, 0, 1, 3))
        .reshape(tok_rows, q_heads * HEAD_SIZE)
        .astype(jnp.bfloat16)
    )
    product = jnp.dot(
        attn,
        lax.all_gather(out_weight, "blk", axis=1, tiled=True),
        preferred_element_type=jnp.float32,
    )
    return lax.psum_scatter(product.astype(jnp.bfloat16), "mp", scatter_dimension=1, tiled=True)


def solution(mesh):
    placed = (
        P("blk", "mp"),
        P("blk", "mp"),
        P("blk", "mp"),
        P("blk", "mp"),
        P("blk", "mp"),
        P("mp", "blk"),
        P(),
    )
    return jax.shard_map(
        per_device, mesh=mesh, in_specs=placed, out_specs=P("blk", "mp"), check_vma=False
    )
```

profile of v0, /device:TPU:2, one launch (start us, length us, event | category | flops | bytes accessed | tf_op | source)
XLA Modules:
  0.0 754.1 jit_solution(11717746178946045109)
XLA Ops:
  6.5 0.7 all-gather.2.cloned.1.call-update
  7.3 1.1 copy.35
  8.5 0.7 copy.37
  9.4 192.3 %all_gather.9 = bf16[2048,128]{1,0:T(8,128)(2,1)S(1)} all-gather(bf16[32,128]{1,0:T(8,128)(2,1)} %param.12), channel_id=1, replica_groups=mesh['blk'=64,'mp'=8] {'blk'}, dimensions={0}, use_global_device_ids=true | all-gather | bytes 532480 | tf_op jit(solution)/shard_map/all_gather | solution.py:79
  201.6 148.2 %all_gather.10 = bf16[2048,128]{1,0:T(8,128)(2,1)S(1)} all-gather(bf16[32,128]{1,0:T(8,128)(2,1)S(1)} %copy-done.2), channel_id=1, replica_groups=mesh['blk'=64,'mp'=8] {'blk'}, dimensions={0}, use_global_device_ids=true | all-gather | bytes 532480 | tf_op jit(solution)/shard_map/all_gather | solution.py:80
  350.4 1.5 bitcast_reduce_fusion
  352.6 1.7 fusion.19
  354.3 2.3 fusion.29
  357.2 280.1 %while.20 = (s32[]{:T(128)}, f32[1,5,256]{2,1,0:T(8,128)S(1)}, f32[1,5,256]{2,1,0:T(8,128)S(1)}, f32[1,5,256,128]{3,2,1,0:T(8,128)S(1)}, bf16[2,256,128]{2,1,0:T...) while((s32[]{:T(128)}, f32[1,5,256]{2,1,0:T(8,128)S(1)}, ...), condition=%wide.region_10.11_spmd.clone, body=%wide.region_6.0_spmd.clone.sunk | while | flops 171328000 | bytes 6847233 | solution.py:103
  357.2 2.2 collective-permute-start
  359.7 16.6 %collective-permute-done = bf16[2,256,128]{2,1,0:T(8,128)(2,1)S(1)} collective-permute-done((bf16[2,256,128]{2,1,0:T(8,128)(2,1)S(1)}, bf16[2,256,128]{2,1,0:T(8,128)(2,1)S(1)}, u32[]{:S(2)}, u32[]{:S(2)}) %collective-permute-start) | collective-permute-done | bytes 131104 | tf_op jit(solution)/shard_map/while/body/eval_jaxpr/ppermute | solution.py:14
  377.6 1.9 collective-permute-start
  379.8 15.2 %collective-permute-done = bf16[2,256,128]{2,1,0:T(8,128)(2,1)S(1)} collective-permute-done((bf16[2,256,128]{2,1,0:T(8,128)(2,1)S(1)}, bf16[2,256,128]{2,1,0:T(8,128)(2,1)S(1)}, u32[]{:S(2)}, u32[]{:S(2)}) %collective-permute-start) | collective-permute-done | bytes 131104 | tf_op jit(solution)/shard_map/while/body/eval_jaxpr/ppermute | solution.py:14
  396.3 1.9 collective-permute-start
  398.5 14.0 %collective-permute-done = bf16[2,256,128]{2,1,0:T(8,128)(2,1)S(1)} collective-permute-done((bf16[2,256,128]{2,1,0:T(8,128)(2,1)S(1)}, bf16[2,256,128]{2,1,0:T(8,128)(2,1)S(1)}, u32[]{:S(2)}, u32[]{:S(2)}) %collective-permute-start) | collective-permute-done | bytes 131104 | tf_op jit(solution)/shard_map/while/body/eval_jaxpr/ppermute | solution.py:14
  413.2 0.6 fusion.66
  413.8 1.9 collective-permute-start
  416.1 13.7 %collective-permute-done = bf16[2,256,128]{2,1,0:T(8,128)(2,1)S(1)} collective-permute-done((bf16[2,256,128]{2,1,0:T(8,128)(2,1)S(1)}, bf16[2,256,128]{2,1,0:T(8,128)(2,1)S(1)}, u32[]{:S(2)}, u32[]{:S(2)}) %collective-permute-start) | collective-permute-done | bytes 131104 | tf_op jit(solution)/shard_map/while/body/eval_jaxpr/ppermute | solution.py:14
  430.4 0.6 fusion.66
  431.0 1.9 collective-permute-start
  433.2 13.7 %collective-permute-done = bf16[2,256,128]{2,1,0:T(8,128)(2,1)S(1)} collective-permute-done((bf16[2,256,128]{2,1,0:T(8,128)(2,1)S(1)}, bf16[2,256,128]{2,1,0:T(8,128)(2,1)S(1)}, u32[]{:S(2)}, u32[]{:S(2)}) %collective-permute-start) | collective-permute-done | bytes 131104 | tf_op jit(solution)/shard_map/while/body/eval_jaxpr/ppermute | solution.py:14
  447.6 0.6 fusion.66
  448.2 1.9 collective-permute-start
  450.4 13.7 %collective-permute-done = bf16[2,256,128]{2,1,0:T(8,128)(2,1)S(1)} collective-permute-done((bf16[2,256,128]{2,1,0:T(8,128)(2,1)S(1)}, bf16[2,256,128]{2,1,0:T(8,128)(2,1)S(1)}, u32[]{:S(2)}, u32[]{:S(2)}) %collective-permute-start) | collective-permute-done | bytes 131104 | tf_op jit(solution)/shard_map/while/body/eval_jaxpr/ppermute | solution.py:14
  465.4 1.9 collective-permute-start
  467.6 13.7 %collective-permute-done = bf16[2,256,128]{2,1,0:T(8,128)(2,1)S(1)} collective-permute-done((bf16[2,256,128]{2,1,0:T(8,128)(2,1)S(1)}, bf16[2,256,128]{2,1,0:T(8,128)(2,1)S(1)}, u32[]{:S(2)}, u32[]{:S(2)}) %collective-permute-start) | collective-permute-done | bytes 131104 | tf_op jit(solution)/shard_map/while/body/eval_jaxpr/ppermute | solution.py:14
  482.6 1.9 collective-permute-start
  484.8 13.7 %collective-permute-done = bf16[2,256,128]{2,1,0:T(8,128)(2,1)S(1)} collective-permute-done((bf16[2,256,128]{2,1,0:T(8,128)(2,1)S(1)}, bf16[2,256,128]{2,1,0:T(8,128)(2,1)S(1)}, u32[]{:S(2)}, u32[]{:S(2)}) %collective-permute-start) | collective-permute-done | bytes 131104 | tf_op jit(solution)/shard_map/while/body/eval_jaxpr/ppermute | solution.py:14
  499.8 1.9 collective-permute-start
  502.0 13.7 %collective-permute-done = bf16[2,256,128]{2,1,0:T(8,128)(2,1)S(1)} collective-permute-done((bf16[2,256,128]{2,1,0:T(8,128)(2,1)S(1)}, bf16[2,256,128]{2,1,0:T(8,128)(2,1)S(1)}, u32[]{:S(2)}, u32[]{:S(2)}) %collective-permute-start) | collective-permute-done | bytes 131104 | tf_op jit(solution)/shard_map/while/body/eval_jaxpr/ppermute | solution.py:14
  517.0 1.9 collective-permute-start
  519.2 13.7 %collective-permute-done = bf16[2,256,128]{2,1,0:T(8,128)(2,1)S(1)} collective-permute-done((bf16[2,256,128]{2,1,0:T(8,128)(2,1)S(1)}, bf16[2,256,128]{2,1,0:T(8,128)(2,1)S(1)}, u32[]{:S(2)}, u32[]{:S(2)}) %collective-permute-start) | collective-permute-done | bytes 131104 | tf_op jit(solution)/shard_map/while/body/eval_jaxpr/ppermute | solution.py:14
  534.1 1.9 collective-permute-start
  536.4 13.7 %collective-permute-done = bf16[2,256,128]{2,1,0:T(8,128)(2,1)S(1)} collective-permute-done((bf16[2,256,128]{2,1,0:T(8,128)(2,1)S(1)}, bf16[2,256,128]{2,1,0:T(8,128)(2,1)S(1)}, u32[]{:S(2)}, u32[]{:S(2)}) %collective-permute-start) | collective-permute-done | bytes 131104 | tf_op jit(solution)/shard_map/while/body/eval_jaxpr/ppermute | solution.py:14
  551.3 1.9 collective-permute-start
  553.6 13.7 %collective-permute-done = bf16[2,256,128]{2,1,0:T(8,128)(2,1)S(1)} collective-permute-done((bf16[2,256,128]{2,1,0:T(8,128)(2,1)S(1)}, bf16[2,256,128]{2,1,0:T(8,128)(2,1)S(1)}, u32[]{:S(2)}, u32[]{:S(2)}) %collective-permute-start) | collective-permute-done | bytes 131104 | tf_op jit(solution)/shard_map/while/body/eval_jaxpr/ppermute | solution.py:14
  568.5 1.9 collective-permute-start
  570.7 13.7 %collective-permute-done = bf16[2,256,128]{2,1,0:T(8,128)(2,1)S(1)} collective-permute-done((bf16[2,256,128]{2,1,0:T(8,128)(2,1)S(1)}, bf16[2,256,128]{2,1,0:T(8,128)(2,1)S(1)}, u32[]{:S(2)}, u32[]{:S(2)}) %collective-permute-start) | collective-permute-done | bytes 131104 | tf_op jit(solution)/shard_map/while/body/eval_jaxpr/ppermute | solution.py:14
  585.7 1.9 collective-permute-start
  587.9 13.7 %collective-permute-done = bf16[2,256,128]{2,1,0:T(8,128)(2,1)S(1)} collective-permute-done((bf16[2,256,128]{2,1,0:T(8,128)(2,1)S(1)}, bf16[2,256,128]{2,1,0:T(8,128)(2,1)S(1)}, u32[]{:S(2)}, u32[]{:S(2)}) %collective-permute-start) | collective-permute-done | bytes 131104 | tf_op jit(solution)/shard_map/while/body/eval_jaxpr/ppermute | solution.py:14
  602.9 1.9 collective-permute-start
  605.1 13.7 %collective-permute-done = bf16[2,256,128]{2,1,0:T(8,128)(2,1)S(1)} collective-permute-done((bf16[2,256,128]{2,1,0:T(8,128)(2,1)S(1)}, bf16[2,256,128]{2,1,0:T(8,128)(2,1)S(1)}, u32[]{:S(2)}, u32[]{:S(2)}) %collective-permute-start) | collective-permute-done | bytes 131104 | tf_op jit(solution)/shard_map/while/body/eval_jaxpr/ppermute | solution.py:14
  620.1 1.9 collective-permute-start
  622.3 13.7 %collective-permute-done = bf16[2,256,128]{2,1,0:T(8,128)(2,1)S(1)} collective-permute-done((bf16[2,256,128]{2,1,0:T(8,128)(2,1)S(1)}, bf16[2,256,128]{2,1,0:T(8,128)(2,1)S(1)}, u32[]{:S(2)}, u32[]{:S(2)}) %collective-permute-start) | collective-permute-done | bytes 131104 | tf_op jit(solution)/shard_map/while/body/eval_jaxpr/ppermute | solution.py:14
  637.6 5.1 convolution_convert_fusion
  642.7 2.6 copy.49
  645.3 100.1 %reduce-scatter.4.cloned.1.call-done = bf16[640,256]{1,0:T(8,128)(2,1)} async-done(((bf16[5120,256]{1,0:T(8,128)(2,1)}), bf16[640,256]{1,0:T(8,128)(2,1)}) %reduce-scatter.4.cloned.1.call-update) | async-done | bytes 327696
  745.4 1.9 copy.50
  (198 shorter events, 24.4 us)
Async XLA Ops:
  6.5 195.1 %copy-start.2 = (bf16[32,128]{1,0:T(8,128)(2,1)S(1)}, bf16[32,128]{1,0:T(8,128)(2,1)}, u32[]{:S(2)}) copy-start(bf16[32,128]{1,0:T(8,128)(2,1)} %param.13) | copy-start | bytes 24580
  6.5 631.1 %all-gather.2.cloned.1.call-start = ((), (), s32[]{:S(2)}) async-start(), calls=%async_computation.1 | async-start | bytes 6656000 | tf_op jit(solution)/shard_map/all_gather | solution.py:113
  7.3 738.1 %reduce-scatter.4.cloned.1.call-start = ((), (), s32[]{:S(2)}) async-start(), calls=%async_computation.2 | async-start | bytes 2949120
  350.4 1.5 copy-start
  354.3 2.4 copy-start.1
  357.2 19.1 %collective-permute-start = (bf16[2,256,128]{2,1,0:T(8,128)(2,1)S(1)}, bf16[2,256,128]{2,1,0:T(8,128)(2,1)S(1)}, u32[]{:S(2)}, u32[]{:S(2)}) collective-permute-start(bf16[2,256,128]{2,1,0:T(8,128)(2,1)S(1)} %get-tuple-element.371), channel_id=1, source_target_pairs={{0,8},{8,16},{16,24},{24,32},{32,40},{40,48},{48,56},{56,64},{64,7... | collective-permute-start | bytes 393224 | tf_op jit(solution)/shard_map/while/body/eval_jaxpr/ppermute | solution.py:14
  377.6 17.4 %collective-permute-start = (bf16[2,256,128]{2,1,0:T(8,128)(2,1)S(1)}, bf16[2,256,128]{2,1,0:T(8,128)(2,1)S(1)}, u32[]{:S(2)}, u32[]{:S(2)}) collective-permute-start(bf16[2,256,128]{2,1,0:T(8,128)(2,1)S(1)} %get-tuple-element.371), channel_id=1, source_target_pairs={{0,8},{8,16},{16,24},{24,32},{32,40},{40,48},{48,56},{56,64},{64,7... | collective-permute-start | bytes 393224 | tf_op jit(solution)/shard_map/while/body/eval_jaxpr/ppermute | solution.py:14
  396.3 16.3 %collective-permute-start = (bf16[2,256,128]{2,1,0:T(8,128)(2,1)S(1)}, bf16[2,256,128]{2,1,0:T(8,128)(2,1)S(1)}, u32[]{:S(2)}, u32[]{:S(2)}) collective-permute-start(bf16[2,256,128]{2,1,0:T(8,128)(2,1)S(1)} %get-tuple-element.371), channel_id=1, source_target_pairs={{0,8},{8,16},{16,24},{24,32},{32,40},{40,48},{48,56},{56,64},{64,7... | collective-permute-start | bytes 393224 | tf_op jit(solution)/shard_map/while/body/eval_jaxpr/ppermute | solution.py:14
  413.8 15.9 %collective-permute-start = (bf16[2,256,128]{2,1,0:T(8,128)(2,1)S(1)}, bf16[2,256,128]{2,1,0:T(8,128)(2,1)S(1)}, u32[]{:S(2)}, u32[]{:S(2)}) collective-permute-start(bf16[2,256,128]{2,1,0:T(8,128)(2,1)S(1)} %get-tuple-element.371), channel_id=1, source_target_pairs={{0,8},{8,16},{16,24},{24,32},{32,40},{40,48},{48,56},{56,64},{64,7... | collective-permute-start | bytes 393224 | tf_op jit(solution)/shard_map/while/body/eval_jaxpr/ppermute | solution.py:14
  431.0 15.9 %collective-permute-start = (bf16[2,256,128]{2,1,0:T(8,128)(2,1)S(1)}, bf16[2,256,128]{2,1,0:T(8,128)(2,1)S(1)}, u32[]{:S(2)}, u32[]{:S(2)}) collective-permute-start(bf16[2,256,128]{2,1,0:T(8,128)(2,1)S(1)} %get-tuple-element.371), channel_id=1, source_target_pairs={{0,8},{8,16},{16,24},{24,32},{32,40},{40,48},{48,56},{56,64},{64,7... | collective-permute-start | bytes 393224 | tf_op jit(solution)/shard_map/while/body/eval_jaxpr/ppermute | solution.py:14
  448.2 15.9 %collective-permute-start = (bf16[2,256,128]{2,1,0:T(8,128)(2,1)S(1)}, bf16[2,256,128]{2,1,0:T(8,128)(2,1)S(1)}, u32[]{:S(2)}, u32[]{:S(2)}) collective-permute-start(bf16[2,256,128]{2,1,0:T(8,128)(2,1)S(1)} %get-tuple-element.371), channel_id=1, source_target_pairs={{0,8},{8,16},{16,24},{24,32},{32,40},{40,48},{48,56},{56,64},{64,7... | collective-permute-start | bytes 393224 | tf_op jit(solution)/shard_map/while/body/eval_jaxpr/ppermute | solution.py:14
  465.4 15.9 %collective-permute-start = (bf16[2,256,128]{2,1,0:T(8,128)(2,1)S(1)}, bf16[2,256,128]{2,1,0:T(8,128)(2,1)S(1)}, u32[]{:S(2)}, u32[]{:S(2)}) collective-permute-start(bf16[2,256,128]{2,1,0:T(8,128)(2,1)S(1)} %get-tuple-element.371), channel_id=1, source_target_pairs={{0,8},{8,16},{16,24},{24,32},{32,40},{40,48},{48,56},{56,64},{64,7... | collective-permute-start | bytes 393224 | tf_op jit(solution)/shard_map/while/body/eval_jaxpr/ppermute | solution.py:14
  482.6 15.9 %collective-permute-start = (bf16[2,256,128]{2,1,0:T(8,128)(2,1)S(1)}, bf16[2,256,128]{2,1,0:T(8,128)(2,1)S(1)}, u32[]{:S(2)}, u32[]{:S(2)}) collective-permute-start(bf16[2,256,128]{2,1,0:T(8,128)(2,1)S(1)} %get-tuple-element.371), channel_id=1, source_target_pairs={{0,8},{8,16},{16,24},{24,32},{32,40},{40,48},{48,56},{56,64},{64,7... | collective-permute-start | bytes 393224 | tf_op jit(solution)/shard_map/while/body/eval_jaxpr/ppermute | solution.py:14
  499.8 15.9 %collective-permute-start = (bf16[2,256,128]{2,1,0:T(8,128)(2,1)S(1)}, bf16[2,256,128]{2,1,0:T(8,128)(2,1)S(1)}, u32[]{:S(2)}, u32[]{:S(2)}) collective-permute-start(bf16[2,256,128]{2,1,0:T(8,128)(2,1)S(1)} %get-tuple-element.371), channel_id=1, source_target_pairs={{0,8},{8,16},{16,24},{24,32},{32,40},{40,48},{48,56},{56,64},{64,7... | collective-permute-start | bytes 393224 | tf_op jit(solution)/shard_map/while/body/eval_jaxpr/ppermute | solution.py:14
  517.0 15.9 %collective-permute-start = (bf16[2,256,128]{2,1,0:T(8,128)(2,1)S(1)}, bf16[2,256,128]{2,1,0:T(8,128)(2,1)S(1)}, u32[]{:S(2)}, u32[]{:S(2)}) collective-permute-start(bf16[2,256,128]{2,1,0:T(8,128)(2,1)S(1)} %get-tuple-element.371), channel_id=1, source_target_pairs={{0,8},{8,16},{16,24},{24,32},{32,40},{40,48},{48,56},{56,64},{64,7... | collective-permute-start | bytes 393224 | tf_op jit(solution)/shard_map/while/body/eval_jaxpr/ppermute | solution.py:14
  534.1 15.9 %collective-permute-start = (bf16[2,256,128]{2,1,0:T(8,128)(2,1)S(1)}, bf16[2,256,128]{2,1,0:T(8,128)(2,1)S(1)}, u32[]{:S(2)}, u32[]{:S(2)}) collective-permute-start(bf16[2,256,128]{2,1,0:T(8,128)(2,1)S(1)} %get-tuple-element.371), channel_id=1, source_target_pairs={{0,8},{8,16},{16,24},{24,32},{32,40},{40,48},{48,56},{56,64},{64,7... | collective-permute-start | bytes 393224 | tf_op jit(solution)/shard_map/while/body/eval_jaxpr/ppermute | solution.py:14
  551.3 15.9 %collective-permute-start = (bf16[2,256,128]{2,1,0:T(8,128)(2,1)S(1)}, bf16[2,256,128]{2,1,0:T(8,128)(2,1)S(1)}, u32[]{:S(2)}, u32[]{:S(2)}) collective-permute-start(bf16[2,256,128]{2,1,0:T(8,128)(2,1)S(1)} %get-tuple-element.371), channel_id=1, source_target_pairs={{0,8},{8,16},{16,24},{24,32},{32,40},{40,48},{48,56},{56,64},{64,7... | collective-permute-start | bytes 393224 | tf_op jit(solution)/shard_map/while/body/eval_jaxpr/ppermute | solution.py:14
  568.5 15.9 %collective-permute-start = (bf16[2,256,128]{2,1,0:T(8,128)(2,1)S(1)}, bf16[2,256,128]{2,1,0:T(8,128)(2,1)S(1)}, u32[]{:S(2)}, u32[]{:S(2)}) collective-permute-start(bf16[2,256,128]{2,1,0:T(8,128)(2,1)S(1)} %get-tuple-element.371), channel_id=1, source_target_pairs={{0,8},{8,16},{16,24},{24,32},{32,40},{40,48},{48,56},{56,64},{64,7... | collective-permute-start | bytes 393224 | tf_op jit(solution)/shard_map/while/body/eval_jaxpr/ppermute | solution.py:14
  585.7 15.9 %collective-permute-start = (bf16[2,256,128]{2,1,0:T(8,128)(2,1)S(1)}, bf16[2,256,128]{2,1,0:T(8,128)(2,1)S(1)}, u32[]{:S(2)}, u32[]{:S(2)}) collective-permute-start(bf16[2,256,128]{2,1,0:T(8,128)(2,1)S(1)} %get-tuple-element.371), channel_id=1, source_target_pairs={{0,8},{8,16},{16,24},{24,32},{32,40},{40,48},{48,56},{56,64},{64,7... | collective-permute-start | bytes 393224 | tf_op jit(solution)/shard_map/while/body/eval_jaxpr/ppermute | solution.py:14
  602.9 15.9 %collective-permute-start = (bf16[2,256,128]{2,1,0:T(8,128)(2,1)S(1)}, bf16[2,256,128]{2,1,0:T(8,128)(2,1)S(1)}, u32[]{:S(2)}, u32[]{:S(2)}) collective-permute-start(bf16[2,256,128]{2,1,0:T(8,128)(2,1)S(1)} %get-tuple-element.371), channel_id=1, source_target_pairs={{0,8},{8,16},{16,24},{24,32},{32,40},{40,48},{48,56},{56,64},{64,7... | collective-permute-start | bytes 393224 | tf_op jit(solution)/shard_map/while/body/eval_jaxpr/ppermute | solution.py:14
  620.1 15.9 %collective-permute-start = (bf16[2,256,128]{2,1,0:T(8,128)(2,1)S(1)}, bf16[2,256,128]{2,1,0:T(8,128)(2,1)S(1)}, u32[]{:S(2)}, u32[]{:S(2)}) collective-permute-start(bf16[2,256,128]{2,1,0:T(8,128)(2,1)S(1)} %get-tuple-element.371), channel_id=1, source_target_pairs={{0,8},{8,16},{16,24},{24,32},{32,40},{40,48},{48,56},{56,64},{64,7... | collective-permute-start | bytes 393224 | tf_op jit(solution)/shard_map/while/body/eval_jaxpr/ppermute | solution.py:14
Sparse Core Ops, SparseCore 0:
  11.8 165.6 all-gather.1
  645.4 99.9 reduce-scatter.3
where the time goes:
time: 756 us; the launch traced here: 754 us
  blocking collectives  341 us (45%)
  waiting for transfers between devices  324 us (43%)
  starting transfers between devices  31.1 us (4%)
  matrix products  25 us (3%)
  between operations  13.6 us (2%)
  other arithmetic  11.1 us (1%)
    ppermute x16, waiting for transfers between devices, passed_along(): return lax.ppermute(block, axis, route)  223 us
    all_gather x1, blocking collectives, per_device(): lax.all_gather(shared_prefix_keys, 'blk', axis=0, tiled=True)  192 us
    all_gather x1, blocking collectives, per_device(): lax.all_gather(shared_prefix_values, 'blk', axis=0, tiled=True)  148 us
    unnamed x3, waiting for transfers between devices  101 us
    ppermute x16, starting transfers between devices, passed_along(): return lax.ppermute(block, axis, route)  31.1 us
  transfers between devices with their start and end apart: 18, of which 17 were waited for; matrix products, arithmetic and copies ran while one was open for 4% of the time, Pallas kernels for 0%

commit v1 on v0

--- a/solution.py
+++ b/solution.py
@@ -1,3 +1,4 @@
+import functools
 import math
 import jax
 import jax.numpy as jnp
@@ -6,6 +7,19 @@
 
 HEAD_SIZE = 128
 MASKED_SCORE = -1e30
+
+
+def return_all_steps_all(block_in, bus_axis, ndim_at):
+    carry_in = jnp.concatenate(
+        lax.all_to_all(
+            jnp.stack([block_in for _ in range(lax.axis_size(bus_axis))]), bus_axis, 0, 0
+        ),
+        ndim_at,
+    )
+    return carry_in
+
+
+groups_render = functools.partial(return_all_steps_all, bus_axis="blk", ndim_at=0)
 
 
 def passed_along(block, axis, distance):
@@ -76,7 +90,7 @@
     )
     carry_state = update(
         start_state,
-        lax.all_gather(shared_prefix_keys, "blk", axis=0, tiled=True),
+        groups_render(shared_prefix_keys),
         lax.all_gather(shared_prefix_values, "blk", axis=0, tiled=True),
         None,
     )

time: 756 us -> 633 us (0.84)
  the two profiles are of different devices: /device:TPU:2 before, /device:TPU:16 now
where the time goes in v1:
time: 633 us; the launch traced here: 631 us
  waiting for transfers between devices  321 us (51%)
  blocking collectives  198 us (31%)
  starting transfers between devices  52.4 us (8%)
  matrix products  25.1 us (4%)
  between operations  13.6 us (2%)
  other arithmetic  11.7 us (2%)
  local copies, waits for them, and re-layouts  7.38 us (1%)
    ppermute x16, waiting for transfers between devices, passed_along(): return lax.ppermute(block, axis, route)  255 us
    all_gather x1, blocking collectives, per_device(): lax.all_gather(shared_prefix_values, 'blk', axis=0, tiled=True)  198 us
    unnamed x3, waiting for transfers between devices  65.8 us
    ppermute x16, starting transfers between devices, passed_along(): return lax.ppermute(block, axis, route)  31 us
    all_to_all x1, starting transfers between devices, return_all_steps_all(): lax.all_to_all(jnp.stack([block_in for _ in range(lax.axis_size(bus_axis)...  21.3 us
  transfers between devices with their start and end apart: 19, of which 17 were waited for; matrix products, arithmetic and copies ran while one was open for 5% of the time, Pallas kernels for 0%

profile of v1, /device:TPU:16, one launch (start us, length us, event | category | flops | bytes accessed | tf_op | source)
XLA Modules:
  0.0 630.5 jit_solution(6799888633840612891)
XLA Ops:
  6.5 1.6 stack.8
  8.2 21.3 %all-to-all-start = ((bf16[64,32,128]{2,1,0:T(8,128)(2,1)}), bf16[64,32,128]{2,1,0:T(8,128)(2,1)S(1)}, u32[]{:S(2)}, u32[]{:S(2)}) async-start(bf16[64,32,128]{2,1,0:T(8,128)(2,1)} %stack.8), calls=%async_computation | async-start | bytes 1048576 | tf_op jit(solution)/shard_map/all_to_all | solution.py:14
  29.5 0.7 all-gather.2.cloned.1.call-update
  31.1 0.7 pad_maximum_fusion
  31.9 197.8 %all_gather.6 = bf16[2048,128]{1,0:T(8,128)(2,1)S(1)} all-gather(bf16[32,128]{1,0:T(8,128)(2,1)S(1)} %copy-done.4), channel_id=1, replica_groups=mesh['blk'=64,'mp'=8] {'blk'}, dimensions={0}, use_global_device_ids=true | all-gather | bytes 532480 | tf_op jit(solution)/shard_map/all_gather | solution.py:94
  230.1 1.5 bitcast_reduce_fusion
  231.9 1.7 fusion.19
  233.6 2.4 fusion.29
  236.9 311.7 %while.20 = (s32[]{:T(128)}, f32[1,5,256]{2,1,0:T(8,128)S(1)}, f32[1,5,256]{2,1,0:T(8,128)S(1)}, f32[1,5,256,128]{3,2,1,0:T(8,128)S(1)}, bf16[2,256,128]{2,1,0:T...) while((s32[]{:T(128)}, f32[1,5,256]{2,1,0:T(8,128)S(1)}, ...), condition=%wide.region_10.11_spmd.clone, body=%wide.region_6.0_spmd.clone.sunk | while | flops 171328000 | bytes 6847233 | solution.py:117
  236.9 2.2 collective-permute-start
  239.5 15.5 %collective-permute-done = bf16[2,256,128]{2,1,0:T(8,128)(2,1)S(1)} collective-permute-done((bf16[2,256,128]{2,1,0:T(8,128)(2,1)S(1)}, bf16[2,256,128]{2,1,0:T(8,128)(2,1)S(1)}, u32[]{:S(2)}, u32[]{:S(2)}) %collective-permute-start) | collective-permute-done | bytes 131104 | tf_op jit(solution)/shard_map/while/body/eval_jaxpr/ppermute | solution.py:28
  256.2 1.9 collective-permute-start
  258.5 15.8 %collective-permute-done = bf16[2,256,128]{2,1,0:T(8,128)(2,1)S(1)} collective-permute-done((bf16[2,256,128]{2,1,0:T(8,128)(2,1)S(1)}, bf16[2,256,128]{2,1,0:T(8,128)(2,1)S(1)}, u32[]{:S(2)}, u32[]{:S(2)}) %collective-permute-start) | collective-permute-done | bytes 131104 | tf_op jit(solution)/shard_map/while/body/eval_jaxpr/ppermute | solution.py:28
  274.9 0.6 fusion.65
  275.5 1.9 collective-permute-start
  277.8 15.8 %collective-permute-done = bf16[2,256,128]{2,1,0:T(8,128)(2,1)S(1)} collective-permute-done((bf16[2,256,128]{2,1,0:T(8,128)(2,1)S(1)}, bf16[2,256,128]{2,1,0:T(8,128)(2,1)S(1)}, u32[]{:S(2)}, u32[]{:S(2)}) %collective-permute-start) | collective-permute-done | bytes 131104 | tf_op jit(solution)/shard_map/while/body/eval_jaxpr/ppermute | solution.py:28
  294.8 1.9 collective-permute-start
  297.1 18.6 %collective-permute-done = bf16[2,256,128]{2,1,0:T(8,128)(2,1)S(1)} collective-permute-done((bf16[2,256,128]{2,1,0:T(8,128)(2,1)S(1)}, bf16[2,256,128]{2,1,0:T(8,128)(2,1)S(1)}, u32[]{:S(2)}, u32[]{:S(2)}) %collective-permute-start) | collective-permute-done | bytes 131104 | tf_op jit(solution)/shard_map/while/body/eval_jaxpr/ppermute | solution.py:28
  316.4 0.6 fusion.65
  317.0 1.9 collective-permute-start
  319.2 15.8 %collective-permute-done = bf16[2,256,128]{2,1,0:T(8,128)(2,1)S(1)} collective-permute-done((bf16[2,256,128]{2,1,0:T(8,128)(2,1)S(1)}, bf16[2,256,128]{2,1,0:T(8,128)(2,1)S(1)}, u32[]{:S(2)}, u32[]{:S(2)}) %collective-permute-start) | collective-permute-done | bytes 131104 | tf_op jit(solution)/shard_map/while/body/eval_jaxpr/ppermute | solution.py:28
  336.3 1.9 collective-permute-start
  338.5 15.8 %collective-permute-done = bf16[2,256,128]{2,1,0:T(8,128)(2,1)S(1)} collective-permute-done((bf16[2,256,128]{2,1,0:T(8,128)(2,1)S(1)}, bf16[2,256,128]{2,1,0:T(8,128)(2,1)S(1)}, u32[]{:S(2)}, u32[]{:S(2)}) %collective-permute-start) | collective-permute-done | bytes 131104 | tf_op jit(solution)/shard_map/while/body/eval_jaxpr/ppermute | solution.py:28
  355.0 0.6 fusion.65
  355.6 1.9 collective-permute-start
  357.8 15.8 %collective-permute-done = bf16[2,256,128]{2,1,0:T(8,128)(2,1)S(1)} collective-permute-done((bf16[2,256,128]{2,1,0:T(8,128)(2,1)S(1)}, bf16[2,256,128]{2,1,0:T(8,128)(2,1)S(1)}, u32[]{:S(2)}, u32[]{:S(2)}) %collective-permute-start) | collective-permute-done | bytes 131104 | tf_op jit(solution)/shard_map/while/body/eval_jaxpr/ppermute | solution.py:28
  374.9 1.9 collective-permute-start
  377.1 15.9 %collective-permute-done = bf16[2,256,128]{2,1,0:T(8,128)(2,1)S(1)} collective-permute-done((bf16[2,256,128]{2,1,0:T(8,128)(2,1)S(1)}, bf16[2,256,128]{2,1,0:T(8,128)(2,1)S(1)}, u32[]{:S(2)}, u32[]{:S(2)}) %collective-permute-start) | collective-permute-done | bytes 131104 | tf_op jit(solution)/shard_map/while/body/eval_jaxpr/ppermute | solution.py:28
  394.3 1.9 collective-permute-start
  396.5 15.8 %collective-permute-done = bf16[2,256,128]{2,1,0:T(8,128)(2,1)S(1)} collective-permute-done((bf16[2,256,128]{2,1,0:T(8,128)(2,1)S(1)}, bf16[2,256,128]{2,1,0:T(8,128)(2,1)S(1)}, u32[]{:S(2)}, u32[]{:S(2)}) %collective-permute-start) | collective-permute-done | bytes 131104 | tf_op jit(solution)/shard_map/while/body/eval_jaxpr/ppermute | solution.py:28
  413.6 1.9 collective-permute-start
  415.8 15.8 %collective-permute-done = bf16[2,256,128]{2,1,0:T(8,128)(2,1)S(1)} collective-permute-done((bf16[2,256,128]{2,1,0:T(8,128)(2,1)S(1)}, bf16[2,256,128]{2,1,0:T(8,128)(2,1)S(1)}, u32[]{:S(2)}, u32[]{:S(2)}) %collective-permute-start) | collective-permute-done | bytes 131104 | tf_op jit(solution)/shard_map/while/body/eval_jaxpr/ppermute | solution.py:28
  432.9 1.9 collective-permute-start
  435.1 15.8 %collective-permute-done = bf16[2,256,128]{2,1,0:T(8,128)(2,1)S(1)} collective-permute-done((bf16[2,256,128]{2,1,0:T(8,128)(2,1)S(1)}, bf16[2,256,128]{2,1,0:T(8,128)(2,1)S(1)}, u32[]{:S(2)}, u32[]{:S(2)}) %collective-permute-start) | collective-permute-done | bytes 131104 | tf_op jit(solution)/shard_map/while/body/eval_jaxpr/ppermute | solution.py:28
  452.2 1.9 collective-permute-start
  454.4 15.8 %collective-permute-done = bf16[2,256,128]{2,1,0:T(8,128)(2,1)S(1)} collective-permute-done((bf16[2,256,128]{2,1,0:T(8,128)(2,1)S(1)}, bf16[2,256,128]{2,1,0:T(8,128)(2,1)S(1)}, u32[]{:S(2)}, u32[]{:S(2)}) %collective-permute-start) | collective-permute-done | bytes 131104 | tf_op jit(solution)/shard_map/while/body/eval_jaxpr/ppermute | solution.py:28
  471.5 1.9 collective-permute-start
  473.7 15.8 %collective-permute-done = bf16[2,256,128]{2,1,0:T(8,128)(2,1)S(1)} collective-permute-done((bf16[2,256,128]{2,1,0:T(8,128)(2,1)S(1)}, bf16[2,256,128]{2,1,0:T(8,128)(2,1)S(1)}, u32[]{:S(2)}, u32[]{:S(2)}) %collective-permute-start) | collective-permute-done | bytes 131104 | tf_op jit(solution)/shard_map/while/body/eval_jaxpr/ppermute | solution.py:28
  490.8 1.9 collective-permute-start
  493.0 15.8 %collective-permute-done = bf16[2,256,128]{2,1,0:T(8,128)(2,1)S(1)} collective-permute-done((bf16[2,256,128]{2,1,0:T(8,128)(2,1)S(1)}, bf16[2,256,128]{2,1,0:T(8,128)(2,1)S(1)}, u32[]{:S(2)}, u32[]{:S(2)}) %collective-permute-start) | collective-permute-done | bytes 131104 | tf_op jit(solution)/shard_map/while/body/eval_jaxpr/ppermute | solution.py:28
  510.1 1.9 collective-permute-start
  512.3 15.8 %collective-permute-done = bf16[2,256,128]{2,1,0:T(8,128)(2,1)S(1)} collective-permute-done((bf16[2,256,128]{2,1,0:T(8,128)(2,1)S(1)}, bf16[2,256,128]{2,1,0:T(8,128)(2,1)S(1)}, u32[]{:S(2)}, u32[]{:S(2)}) %collective-permute-start) | collective-permute-done | bytes 131104 | tf_op jit(solution)/shard_map/while/body/eval_jaxpr/ppermute | solution.py:28
  529.4 1.9 collective-permute-start
  531.6 15.8 %collective-permute-done = bf16[2,256,128]{2,1,0:T(8,128)(2,1)S(1)} collective-permute-done((bf16[2,256,128]{2,1,0:T(8,128)(2,1)S(1)}, bf16[2,256,128]{2,1,0:T(8,128)(2,1)S(1)}, u32[]{:S(2)}, u32[]{:S(2)}) %collective-permute-start) | collective-permute-done | bytes 131104 | tf_op jit(solution)/shard_map/while/body/eval_jaxpr/ppermute | solution.py:28
  549.0 5.1 convolution_convert_fusion
  554.1 2.6 copy.49
  556.7 65.1 %reduce-scatter.4.cloned.1.call-done = bf16[640,256]{1,0:T(8,128)(2,1)} async-done(((bf16[5120,256]{1,0:T(8,128)(2,1)}), bf16[640,256]{1,0:T(8,128)(2,1)}) %reduce-scatter.4.cloned.1.call-update) | async-done | bytes 327696
  621.8 1.9 copy.50
  (206 shorter events, 25.1 us)
Async XLA Ops:
  6.5 23.7 %copy-start = (bf16[256,640]{1,0:T(8,128)(2,1)S(1)}, bf16[256,640]{1,0:T(8,128)(2,1)}, u32[]{:S(2)}) copy-start(bf16[256,640]{1,0:T(8,128)(2,1)} %param.9) | copy-start | bytes 983044
  6.5 23.9 %copy-start.5 = (s32[16]{0:T(128)S(1)}, s32[16]{0:T(128)}, u32[]{:S(2)}) copy-start(s32[16]{0:T(128)} %param.15) | copy-start | bytes 196
  8.2 22.9 %copy-start.1 = (bf16[256,128]{1,0:T(8,128)(2,1)S(1)}, bf16[256,128]{1,0:T(8,128)(2,1)}, u32[]{:S(2)}) copy-start(bf16[256,128]{1,0:T(8,128)(2,1)} %param.10) | copy-start | bytes 196612
  8.2 22.9 %copy-start.2 = (bf16[256,128]{1,0:T(8,128)(2,1)S(1)}, bf16[256,128]{1,0:T(8,128)(2,1)}, u32[]{:S(2)}) copy-start(bf16[256,128]{1,0:T(8,128)(2,1)} %param.11) | copy-start | bytes 196612
  8.2 23.7 %copy-start.4 = (bf16[32,128]{1,0:T(8,128)(2,1)S(1)}, bf16[32,128]{1,0:T(8,128)(2,1)}, u32[]{:S(2)}) copy-start(bf16[32,128]{1,0:T(8,128)(2,1)} %param.13) | copy-start | bytes 24580
  8.2 222.0 %all-to-all-start = ((bf16[64,32,128]{2,1,0:T(8,128)(2,1)}), bf16[64,32,128]{2,1,0:T(8,128)(2,1)S(1)}, u32[]{:S(2)}, u32[]{:S(2)}) async-start(bf16[64,32,128]{2,1,0:T(8,128)(2,1)} %stack.8), calls=%async_computation | async-start | bytes 1048576 | tf_op jit(solution)/shard_map/all_to_all | solution.py:14
  29.5 519.5 %all-gather.2.cloned.1.call-start = ((), (), s32[]{:S(2)}) async-start(), calls=%async_computation.2 | async-start | bytes 6656000 | tf_op jit(solution)/shard_map/all_gather | solution.py:127
  30.2 591.6 %reduce-scatter.4.cloned.1.call-start = ((), (), s32[]{:S(2)}) async-start(), calls=%async_computation.3 | async-start | bytes 2949120
  236.0 0.9 copy-start.3
  236.9 18.0 %collective-permute-start = (bf16[2,256,128]{2,1,0:T(8,128)(2,1)S(1)}, bf16[2,256,128]{2,1,0:T(8,128)(2,1)S(1)}, u32[]{:S(2)}, u32[]{:S(2)}) collective-permute-start(bf16[2,256,128]{2,1,0:T(8,128)(2,1)S(1)} %get-tuple-element.371), channel_id=1, source_target_pairs={{0,8},{8,16},{16,24},{24,32},{32,40},{40,48},{48,56},{56,64},{64,7... | collective-permute-start | bytes 393224 | tf_op jit(solution)/shard_map/while/body/eval_jaxpr/ppermute | solution.py:28
  256.2 18.0 %collective-permute-start = (bf16[2,256,128]{2,1,0:T(8,128)(2,1)S(1)}, bf16[2,256,128]{2,1,0:T(8,128)(2,1)S(1)}, u32[]{:S(2)}, u32[]{:S(2)}) collective-permute-start(bf16[2,256,128]{2,1,0:T(8,128)(2,1)S(1)} %get-tuple-element.371), channel_id=1, source_target_pairs={{0,8},{8,16},{16,24},{24,32},{32,40},{40,48},{48,56},{56,64},{64,7... | collective-permute-start | bytes 393224 | tf_op jit(solution)/shard_map/while/body/eval_jaxpr/ppermute | solution.py:28
  275.5 18.0 %collective-permute-start = (bf16[2,256,128]{2,1,0:T(8,128)(2,1)S(1)}, bf16[2,256,128]{2,1,0:T(8,128)(2,1)S(1)}, u32[]{:S(2)}, u32[]{:S(2)}) collective-permute-start(bf16[2,256,128]{2,1,0:T(8,128)(2,1)S(1)} %get-tuple-element.371), channel_id=1, source_target_pairs={{0,8},{8,16},{16,24},{24,32},{32,40},{40,48},{48,56},{56,64},{64,7... | collective-permute-start | bytes 393224 | tf_op jit(solution)/shard_map/while/body/eval_jaxpr/ppermute | solution.py:28
  294.8 20.8 %collective-permute-start = (bf16[2,256,128]{2,1,0:T(8,128)(2,1)S(1)}, bf16[2,256,128]{2,1,0:T(8,128)(2,1)S(1)}, u32[]{:S(2)}, u32[]{:S(2)}) collective-permute-start(bf16[2,256,128]{2,1,0:T(8,128)(2,1)S(1)} %get-tuple-element.371), channel_id=1, source_target_pairs={{0,8},{8,16},{16,24},{24,32},{32,40},{40,48},{48,56},{56,64},{64,7... | collective-permute-start | bytes 393224 | tf_op jit(solution)/shard_map/while/body/eval_jaxpr/ppermute | solution.py:28
  317.0 18.0 %collective-permute-start = (bf16[2,256,128]{2,1,0:T(8,128)(2,1)S(1)}, bf16[2,256,128]{2,1,0:T(8,128)(2,1)S(1)}, u32[]{:S(2)}, u32[]{:S(2)}) collective-permute-start(bf16[2,256,128]{2,1,0:T(8,128)(2,1)S(1)} %get-tuple-element.371), channel_id=1, source_target_pairs={{0,8},{8,16},{16,24},{24,32},{32,40},{40,48},{48,56},{56,64},{64,7... | collective-permute-start | bytes 393224 | tf_op jit(solution)/shard_map/while/body/eval_jaxpr/ppermute | solution.py:28
  336.3 18.0 %collective-permute-start = (bf16[2,256,128]{2,1,0:T(8,128)(2,1)S(1)}, bf16[2,256,128]{2,1,0:T(8,128)(2,1)S(1)}, u32[]{:S(2)}, u32[]{:S(2)}) collective-permute-start(bf16[2,256,128]{2,1,0:T(8,128)(2,1)S(1)} %get-tuple-element.371), channel_id=1, source_target_pairs={{0,8},{8,16},{16,24},{24,32},{32,40},{40,48},{48,56},{56,64},{64,7... | collective-permute-start | bytes 393224 | tf_op jit(solution)/shard_map/while/body/eval_jaxpr/ppermute | solution.py:28
  355.6 18.0 %collective-permute-start = (bf16[2,256,128]{2,1,0:T(8,128)(2,1)S(1)}, bf16[2,256,128]{2,1,0:T(8,128)(2,1)S(1)}, u32[]{:S(2)}, u32[]{:S(2)}) collective-permute-start(bf16[2,256,128]{2,1,0:T(8,128)(2,1)S(1)} %get-tuple-element.371), channel_id=1, source_target_pairs={{0,8},{8,16},{16,24},{24,32},{32,40},{40,48},{48,56},{56,64},{64,7... | collective-permute-start | bytes 393224 | tf_op jit(solution)/shard_map/while/body/eval_jaxpr/ppermute | solution.py:28
  374.9 18.1 %collective-permute-start = (bf16[2,256,128]{2,1,0:T(8,128)(2,1)S(1)}, bf16[2,256,128]{2,1,0:T(8,128)(2,1)S(1)}, u32[]{:S(2)}, u32[]{:S(2)}) collective-permute-start(bf16[2,256,128]{2,1,0:T(8,128)(2,1)S(1)} %get-tuple-element.371), channel_id=1, source_target_pairs={{0,8},{8,16},{16,24},{24,32},{32,40},{40,48},{48,56},{56,64},{64,7... | collective-permute-start | bytes 393224 | tf_op jit(solution)/shard_map/while/body/eval_jaxpr/ppermute | solution.py:28
  394.3 18.0 %collective-permute-start = (bf16[2,256,128]{2,1,0:T(8,128)(2,1)S(1)}, bf16[2,256,128]{2,1,0:T(8,128)(2,1)S(1)}, u32[]{:S(2)}, u32[]{:S(2)}) collective-permute-start(bf16[2,256,128]{2,1,0:T(8,128)(2,1)S(1)} %get-tuple-element.371), channel_id=1, source_target_pairs={{0,8},{8,16},{16,24},{24,32},{32,40},{40,48},{48,56},{56,64},{64,7... | collective-permute-start | bytes 393224 | tf_op jit(solution)/shard_map/while/body/eval_jaxpr/ppermute | solution.py:28
  413.6 18.0 %collective-permute-start = (bf16[2,256,128]{2,1,0:T(8,128)(2,1)S(1)}, bf16[2,256,128]{2,1,0:T(8,128)(2,1)S(1)}, u32[]{:S(2)}, u32[]{:S(2)}) collective-permute-start(bf16[2,256,128]{2,1,0:T(8,128)(2,1)S(1)} %get-tuple-element.371), channel_id=1, source_target_pairs={{0,8},{8,16},{16,24},{24,32},{32,40},{40,48},{48,56},{56,64},{64,7... | collective-permute-start | bytes 393224 | tf_op jit(solution)/shard_map/while/body/eval_jaxpr/ppermute | solution.py:28
  432.9 18.0 %collective-permute-start = (bf16[2,256,128]{2,1,0:T(8,128)(2,1)S(1)}, bf16[2,256,128]{2,1,0:T(8,128)(2,1)S(1)}, u32[]{:S(2)}, u32[]{:S(2)}) collective-permute-start(bf16[2,256,128]{2,1,0:T(8,128)(2,1)S(1)} %get-tuple-element.371), channel_id=1, source_target_pairs={{0,8},{8,16},{16,24},{24,32},{32,40},{40,48},{48,56},{56,64},{64,7... | collective-permute-start | bytes 393224 | tf_op jit(solution)/shard_map/while/body/eval_jaxpr/ppermute | solution.py:28
  452.2 18.0 %collective-permute-start = (bf16[2,256,128]{2,1,0:T(8,128)(2,1)S(1)}, bf16[2,256,128]{2,1,0:T(8,128)(2,1)S(1)}, u32[]{:S(2)}, u32[]{:S(2)}) collective-permute-start(bf16[2,256,128]{2,1,0:T(8,128)(2,1)S(1)} %get-tuple-element.371), channel_id=1, source_target_pairs={{0,8},{8,16},{16,24},{24,32},{32,40},{40,48},{48,56},{56,64},{64,7... | collective-permute-start | bytes 393224 | tf_op jit(solution)/shard_map/while/body/eval_jaxpr/ppermute | solution.py:28
  471.5 18.0 %collective-permute-start = (bf16[2,256,128]{2,1,0:T(8,128)(2,1)S(1)}, bf16[2,256,128]{2,1,0:T(8,128)(2,1)S(1)}, u32[]{:S(2)}, u32[]{:S(2)}) collective-permute-start(bf16[2,256,128]{2,1,0:T(8,128)(2,1)S(1)} %get-tuple-element.371), channel_id=1, source_target_pairs={{0,8},{8,16},{16,24},{24,32},{32,40},{40,48},{48,56},{56,64},{64,7... | collective-permute-start | bytes 393224 | tf_op jit(solution)/shard_map/while/body/eval_jaxpr/ppermute | solution.py:28
  490.8 18.0 %collective-permute-start = (bf16[2,256,128]{2,1,0:T(8,128)(2,1)S(1)}, bf16[2,256,128]{2,1,0:T(8,128)(2,1)S(1)}, u32[]{:S(2)}, u32[]{:S(2)}) collective-permute-start(bf16[2,256,128]{2,1,0:T(8,128)(2,1)S(1)} %get-tuple-element.371), channel_id=1, source_target_pairs={{0,8},{8,16},{16,24},{24,32},{32,40},{40,48},{48,56},{56,64},{64,7... | collective-permute-start | bytes 393224 | tf_op jit(solution)/shard_map/while/body/eval_jaxpr/ppermute | solution.py:28
  510.1 18.0 %collective-permute-start = (bf16[2,256,128]{2,1,0:T(8,128)(2,1)S(1)}, bf16[2,256,128]{2,1,0:T(8,128)(2,1)S(1)}, u32[]{:S(2)}, u32[]{:S(2)}) collective-permute-start(bf16[2,256,128]{2,1,0:T(8,128)(2,1)S(1)} %get-tuple-element.371), channel_id=1, source_target_pairs={{0,8},{8,16},{16,24},{24,32},{32,40},{40,48},{48,56},{56,64},{64,7... | collective-permute-start | bytes 393224 | tf_op jit(solution)/shard_map/while/body/eval_jaxpr/ppermute | solution.py:28
  529.4 18.0 %collective-permute-start = (bf16[2,256,128]{2,1,0:T(8,128)(2,1)S(1)}, bf16[2,256,128]{2,1,0:T(8,128)(2,1)S(1)}, u32[]{:S(2)}, u32[]{:S(2)}) collective-permute-start(bf16[2,256,128]{2,1,0:T(8,128)(2,1)S(1)} %get-tuple-element.371), channel_id=1, source_target_pairs={{0,8},{8,16},{16,24},{24,32},{32,40},{40,48},{48,56},{56,64},{64,7... | collective-permute-start | bytes 393224 | tf_op jit(solution)/shard_map/while/body/eval_jaxpr/ppermute | solution.py:28
Sparse Core Ops, SparseCore 0:
  34.8 166.9 all-gather.1
  556.8 64.9 reduce-scatter.3
